TPU v7x, 32 devices: a whole 2x2x4 slice. The times are simulated.
32 devices in a mesh: rows: 16 (over z, y, x), cov: 2 (over core).
Axes of the slice: x: 2, y: 2, z: 4, core: 2. Of those that a mesh axis runs over, the one named last changes fastest.
Arguments:
- design: bfloat16 [49152, 1024], P('rows', 'cov')
- tract_id: int32 [49152], P('rows'), may hold values from 0 to 21247, as said below
- outcome: int32 [49152], P('rows'), may hold values 0 or 1
- omega: float32 [49152], P('rows'), may hold values from 0.05 to 0.5
- effects_old: float32 [21248], P('rows'), may hold values from -6 to 6
- normal_coef: float32 [1024], P('cov'), may hold values from -6 to 6
- normal_tract: float32 [21248], P('rows'), may hold values from -6 to 6
Outputs:
- beta: float32 [1024], P('cov')
- effects: float32 [21248], P('rows')
Inputs may be any that keep to these rules, and one draw needn't show every extreme that they name: `tract_id`: A record on the device with index d along rows names a tract from (d - 1) * 1328 to (d + 2) * 1328 - 1, and also from 0 at d = 0 and up to 21247 at the last index; every device other than the first and last names both ends of its range. Some tracts hold many records and some none.
All inputs are finite; a program needn't handle non-finite values. No bound on the sum of `outcome` on one device may be relied on, other than what follows from the above.
Results may differ from a plain program's by a relative error of at most 0.0023.
Values may be sent and summed in bfloat16 or wider, within the bound.
No kernel may reach another device: no remote copies, remote signals or barrier semaphores. Data moves between devices by JAX's collectives and lax.ppermute only.
A program may use at most 128 MiB of HBM per device.

v0:
```python
import jax
import jax.numpy as jnp
from jax import lax
from jax.sharding import PartitionSpec as P

prior_precision = 1.0
tract_precision = 1.0


def extended(block, sides, width):
    for axis, dim in sides:
        count = lax.axis_size(axis)
        forward = [(i, i + 1) for i in range(count - 1)]
        backward = [(target, source) for source, target in forward]
        low = lax.ppermute(
            lax.slice_in_dim(block, block.shape[dim] - width, None, axis=dim), axis, forward
        )
        high = lax.ppermute(lax.slice_in_dim(block, 0, width, axis=dim), axis, backward)
        block = jnp.concatenate([low, block, high], axis=dim)
    return block


def from_behind(block, axis, distance):
    devices = range(lax.axis_size(axis))
    route = [(i - distance, i) for i in devices if i - distance in devices]
    return lax.ppermute(block, axis, route)


def contract_rows(left, right):
    return lax.dot_general(
        left, right, (((0,), (0,)), ((), ())), preferred_element_type=jnp.float32
    )


def local(design, tract_id, outcome, omega, effects_old, normal_coef, normal_tract):
    columns = design.shape[1]
    tract_dev = effects_old.shape[0]
    kappa = outcome.astype(jnp.float32) - 0.5
    window = extended(effects_old, (("rows", 0),), tract_dev)
    local_id = tract_id - (lax.axis_index("rows") - 1) * tract_dev
    effect_row = jnp.take(window, local_id)
    resid = (kappa - omega * effect_row).astype(jnp.bfloat16)
    offset = lax.axis_index("cov") * columns
    weighted = (omega[:, None] * design).astype(jnp.bfloat16)
    gram_block = contract_rows(lax.all_gather(design, "cov", axis=1, tiled=True), weighted)
    rhs_block = contract_rows(design, resid)
    gram_block, rhs_block = lax.psum((gram_block, rhs_block), "rows")
    gram, rhs, noise = (
        lax.all_gather(gram_block, "cov", axis=1, tiled=True),
        lax.all_gather(rhs_block, "cov", axis=0, tiled=True),
        lax.all_gather(normal_coef, "cov", axis=0, tiled=True),
    )
    order = gram.shape[0]
    precision = 0.5 * (gram + gram.T) + prior_precision * jnp.eye(order, dtype=jnp.float32)
    lower = jnp.linalg.cholesky(precision)
    inner = jax.scipy.linalg.solve_triangular(lower, rhs, lower=True) + noise
    beta = jax.scipy.linalg.solve_triangular(lower, inner, trans=1, lower=True)
    beta_b = beta.astype(jnp.bfloat16)
    beta_own = lax.dynamic_slice_in_dim(beta, offset, columns)
    own_coef = lax.dynamic_slice_in_dim(beta_b, offset, columns)
    partial_eta = jnp.dot(design, own_coef, preferred_element_type=jnp.float32)
    eta = lax.psum(partial_eta, "cov")
    contrib = kappa - omega * eta
    weight_sums = jax.ops.segment_sum(omega, local_id, num_segments=3 * tract_dev)
    resid_sums = jax.ops.segment_sum(contrib, local_id, num_segments=3 * tract_dev)
    from_above = from_behind((weight_sums[:tract_dev], resid_sums[:tract_dev]), "rows", -1)
    from_below = from_behind((weight_sums[2 * tract_dev :], resid_sums[2 * tract_dev :]), "rows", 1)
    weight_total = weight_sums[tract_dev : 2 * tract_dev] + from_above[0] + from_below[0]
    resid_total = resid_sums[tract_dev : 2 * tract_dev] + from_above[1] + from_below[1]
    prec = tract_precision + weight_total
    effects = resid_total / prec + normal_tract * lax.rsqrt(prec)
    return (beta_own, effects)


def solution(mesh):
    placed = (P("rows", "cov"), P("rows"), P("rows"), P("rows"), P("rows"), P("cov"), P("rows"))
    return jax.shard_map(
        local, mesh=mesh, in_specs=placed, out_specs=(P("cov"), P("rows")), check_vma=False
    )
```

profile of v0, /device:TPU:8, one launch (start us, length us, event | category | flops | bytes accessed | tf_op | source)
XLA Modules:
  0.0 675.4 jit_solution(14951612070403746616)
XLA Ops:
  7.9 19.8 %all-gather.5.cloned.1.call-done = bf16[3072,1024]{1,0:T(8,128)(2,1)} async-done(((bf16[3072,512]{1,0:T(8,128)(2,1)}), bf16[3072,1024]{1,0:T(8,128)(2,1)}) %all-gather.5.cloned.1.call-update) | async-done | bytes 6291472 | tf_op jit(solution)/shard_map/all_gather | solution.py:45
  27.8 8.6 %fusion.5 = f32[1024,512]{0,1:T(8,128)} fusion(bf16[3072,1024]{1,0:T(8,128)(2,1)} %all-gather.5.cloned.1.call-done, bf16[3072,512]{1,0:T(8,128)(2,1)} %param.7, f32[3072]{0:T(1024)} %param.10), kind=kOutput, calls=%fused_computation.16 | convolution fusion | flops 3225944064 | bytes 11546624 | tf_op jit(solution)/shard_map/dot_general | solution.py:30
  36.5 126.8 %all-reduce.3.cloned.1.call-done = f32[1024,512]{0,1:T(8,128)} async-done(((f32[1024,512]{0,1:T(8,128)}), f32[1024,512]{0,1:T(8,128)}) %all-reduce.3.cloned.1.call-update) | async-done | bytes 2097168 | tf_op jit(solution)/shard_map/psum | solution.py:47
  163.3 3.4 collective-permute-start
  166.7 4.3 collective-permute-start.1
  171.0 16.6 %scatter_custom_fusion.1 = f32[3984]{0:T(1024)S(1)} fusion(s32[3072]{0:T(1024)S(1)} %get-tuple-element.19, f32[3072]{0:T(1024)S(1)} %copy-done.5, f32[]{:T(128)} %constant.307.clone.1), kind=kCustom, calls=%fused_computation.218 | custom fusion | flops 3072 | bytes 15940 | tf_op jit(solution)/shard_map/scatter-add | solution.py:64
  188.3 2.6 collective-permute-start.4
  190.9 3.2 collective-permute-start.5
  196.7 17.4 %gather_fusion = f32[3072]{0:T(1024)S(1)} fusion(f32[3984]{0:T(1024)S(1)} %concatenate.57, s32[3072]{0:T(1024)S(1)} %get-tuple-element.18), kind=kCustom, calls=%fused_computation | custom fusion | bytes 36864 | tf_op jit(solution)/shard_map/jit(_take)/gather | solution.py:41
  214.7 31.9 %psum.22 = f32[512]{0:T(512)S(1)} all-reduce(f32[512]{0:T(512)S(1)} %bitcast.336), channel_id=1, replica_groups=mesh['rows'=16,'cov'=2] {'rows'}, use_global_device_ids=true, to_apply=%region_17.18 | all-reduce | flops 512 | bytes 4096 | tf_op jit(solution)/shard_map/psum | solution.py:47
  248.4 5.4 copy.13
  253.8 6.9 %fusion.2 = f32[1024,1024]{1,0:T(8,128)} fusion(f32[1024,1024]{1,0:T(8,128)} %copy.13, f32[1024,1024]{0,1:T(8,128)} %all-gather.7.cloned.1.call-done), kind=kLoop, calls=%fused_computation.11 | loop fusion | flops 5242880 | bytes 12582912 | tf_op jit(solution)/shard_map/add | solution.py:54
  260.6 5.8 copy.14
  266.5 4.4 fusion
  272.9 11.7 %cholesky.223 = f32[128,128]{1,0:T(8,128)S(1)} custom-call(f32[128,128]{1,0:T(8,128)S(1)} %cholesky.580), custom_call_target="Cholesky" | custom-call | tf_op jit(solution)/shard_map/jit(cholesky)/cholesky | solution.py:55
  285.2 2.5 cholesky.255
  287.7 9.8 %custom-call.66 = f32[1,128,128]{1,2,0:T(8,128)S(1)} custom-call(f32[1,128,128]{2,1,0:T(8,128)S(1)} %get-tuple-element.43), custom_call_target="InvertDiagBlocksLowerTriangular" | custom-call | tf_op jit(solution)/shard_map/jit(cholesky)/cholesky | solution.py:55
  297.5 2.4 constant_dynamic-update-slice_fusion.57
  302.3 11.8 %cholesky.244 = f32[128,128]{1,0:T(8,128)S(1)} custom-call(f32[128,128]{1,0:T(8,128)S(1)} %cholesky.584), custom_call_target="Cholesky" | custom-call | tf_op jit(solution)/shard_map/jit(cholesky)/cholesky | solution.py:55
  315.3 9.8 %custom-call.67 = f32[1,128,128]{1,2,0:T(8,128)S(1)} custom-call(f32[1,128,128]{2,1,0:T(8,128)S(1)} %get-tuple-element.40), custom_call_target="InvertDiagBlocksLowerTriangular" | custom-call | tf_op jit(solution)/shard_map/jit(cholesky)/cholesky | solution.py:55
  330.1 13.2 %cholesky.468 = f32[128,128]{1,0:T(8,128)} custom-call(f32[128,128]{1,0:T(8,128)} %cholesky.589), custom_call_target="Cholesky" | custom-call | tf_op jit(solution)/shard_map/jit(cholesky)/cholesky | solution.py:55
  345.4 11.3 %custom-call.68 = f32[1,128,128]{1,2,0:T(8,128)} custom-call(f32[1,128,128]{2,1,0:T(8,128)} %get-tuple-element.37), custom_call_target="InvertDiagBlocksLowerTriangular" | custom-call | tf_op jit(solution)/shard_map/jit(cholesky)/cholesky | solution.py:55
  358.7 2.3 convolution_subtract_fusion.2
  361.1 12.5 %cholesky.487 = f32[128,128]{1,0:T(8,128)} custom-call(f32[128,128]{1,0:T(8,128)S(1)} %cholesky.594), custom_call_target="Cholesky" | custom-call | tf_op jit(solution)/shard_map/jit(cholesky)/cholesky | solution.py:55
  375.7 10.4 %custom-call.69 = f32[1,128,128]{1,2,0:T(8,128)} custom-call(f32[1,128,128]{2,1,0:T(8,128)S(1)} %get-tuple-element.34), custom_call_target="InvertDiagBlocksLowerTriangular" | custom-call | tf_op jit(solution)/shard_map/jit(cholesky)/cholesky | solution.py:55
  388.1 2.3 convolution_subtract_fusion.3
  390.4 11.7 %cholesky.506 = f32[128,128]{1,0:T(8,128)S(1)} custom-call(f32[128,128]{1,0:T(8,128)S(1)} %cholesky.599), custom_call_target="Cholesky" | custom-call | tf_op jit(solution)/shard_map/jit(cholesky)/cholesky | solution.py:55
  403.4 10.2 %custom-call.70 = f32[1,128,128]{1,2,0:T(8,128)S(1)} custom-call(f32[1,128,128]{2,1,0:T(8,128)S(1)} %get-tuple-element.31), custom_call_target="InvertDiagBlocksLowerTriangular" | custom-call | tf_op jit(solution)/shard_map/jit(cholesky)/cholesky | solution.py:55
  416.9 11.7 %cholesky.526 = f32[128,128]{1,0:T(8,128)S(1)} custom-call(f32[128,128]{1,0:T(8,128)S(1)} %cholesky.604), custom_call_target="Cholesky" | custom-call | tf_op jit(solution)/shard_map/jit(cholesky)/cholesky | solution.py:55
  429.9 9.8 %custom-call.71 = f32[1,128,128]{1,2,0:T(8,128)S(1)} custom-call(f32[1,128,128]{2,1,0:T(8,128)S(1)} %get-tuple-element.28), custom_call_target="InvertDiagBlocksLowerTriangular" | custom-call | tf_op jit(solution)/shard_map/jit(cholesky)/cholesky | solution.py:55
  442.7 11.9 %cholesky.546 = f32[128,128]{1,0:T(8,128)S(1)} custom-call(f32[128,128]{1,0:T(8,128)S(1)} %cholesky.609), custom_call_target="Cholesky" | custom-call | tf_op jit(solution)/shard_map/jit(cholesky)/cholesky | solution.py:55
  455.9 9.8 %custom-call.72 = f32[1,128,128]{1,2,0:T(8,128)S(1)} custom-call(f32[1,128,128]{2,1,0:T(8,128)S(1)} %get-tuple-element.25), custom_call_target="InvertDiagBlocksLowerTriangular" | custom-call | tf_op jit(solution)/shard_map/jit(cholesky)/cholesky | solution.py:55
  468.3 11.7 %cholesky.564 = f32[128,128]{1,0:T(8,128)S(1)} custom-call(f32[128,128]{1,0:T(8,128)S(1)} %convolution_subtract_fusion.6), custom_call_target="Cholesky" | custom-call | tf_op jit(solution)/shard_map/jit(cholesky)/cholesky | solution.py:55
  486.9 4.8 select_select_fusion
  491.7 28.1 %while.1 = (s32[]{:T(128)}, f32[1024,1024]{1,0:T(8,128)}, s32[8,2]{0,1:T(2,128)S(1)}, f32[8,128,128]{2,1,0:T(8,128)}, s32[]{:T(128)}) while((s32[]{:T(128)}, f32[1024,1024]{1,0:T(8,128)}, s32[8,2]{0,1:T(2,128)S(1)}, f32[8,128,128]{2,1,0:T(8,128)}, s32[]{:T(128)}) %tuple.67), condition=%wide.while_cond, body=%wide.while_body.sunk | while | flops 2 | bytes 132705 | solution.py:57
  492.4 2.9 bitcast_dynamic-update-slice_fusion.2
  495.9 2.9 bitcast_dynamic-update-slice_fusion.2
  499.4 2.9 bitcast_dynamic-update-slice_fusion.2
  503.0 2.9 bitcast_dynamic-update-slice_fusion.2
  506.5 2.9 bitcast_dynamic-update-slice_fusion.2
  510.0 2.9 bitcast_dynamic-update-slice_fusion.2
  513.5 2.9 bitcast_dynamic-update-slice_fusion.2
  517.0 2.8 bitcast_dynamic-update-slice_fusion.2
  519.9 80.3 %custom-call.73 = f32[8,128,128]{1,2,0:T(8,128)} custom-call(f32[8,128,128]{2,1,0:T(8,128)} %get-tuple-element.9), custom_call_target="InvertDiagBlocksLowerTriangular" | custom-call | tf_op jit(solution)/shard_map/jit(_solve_triangular)/triangular_solve | solution.py:57
  635.5 3.3 psum.23
  638.8 16.7 %scatter_custom_fusion = f32[3984]{0:T(1024)S(1)} fusion(s32[3072]{0:T(1024)} %copy-done.8, f32[3072]{0:T(1024)S(1)} %multiply_subtract_fusion, f32[]{:T(128)} %constant.307.clone.1), kind=kCustom, calls=%fused_computation.220 | custom fusion | flops 3072 | bytes 16448 | tf_op jit(solution)/shard_map/scatter-add | solution.py:65
  655.6 4.3 collective-permute-start.2
  661.8 5.4 collective-permute-done.3
  (167 shorter events, 84.3 us)
Async XLA Ops:
  7.2 20.6 %all-gather.5.cloned.1.call-start = ((), (), s32[]{:S(2)}) async-start(), calls=%async_computation | async-start | bytes 9437184 | tf_op jit(solution)/shard_map/all_gather | solution.py:45
  7.9 155.4 %all-reduce.3.cloned.1.call-start = ((), (), s32[]{:S(2)}) async-start(), calls=%async_computation.1 | async-start | bytes 4194304 | tf_op jit(solution)/shard_map/psum | solution.py:47
  36.4 126.9 %copy-start.11 = (f32[1328]{0:T(1024)S(1)}, f32[1328]{0:T(1024)}, u32[]{:S(2)}) copy-start(f32[1328]{0:T(1024)} %param.11) | copy-start | bytes 15940
  36.4 134.6 %copy-start.10 = (s32[3072]{0:T(1024)S(1)}, s32[3072]{0:T(1024)}, u32[]{:S(2)}) copy-start(s32[3072]{0:T(1024)} %param.8) | copy-start | bytes 36868
  36.4 134.6 %copy-start.5 = (f32[3072]{0:T(1024)S(1)}, f32[3072]{0:T(1024)}, u32[]{:S(2)}) copy-start(f32[3072]{0:T(1024)} %param.10) | copy-start | bytes 36868
  36.4 158.3 %copy-start.16 = (f32[512]{0:T(512)S(1)}, f32[512]{0:T(512)}, u32[]{:S(2)}) copy-start(f32[512]{0:T(512)} %param.12) | copy-start | bytes 6148
  36.4 212.0 %all-gather.7.cloned.1.call-start = ((), (), s32[]{:S(2)}) async-start(), calls=%async_computation.2 | async-start | bytes 6291456 | tf_op jit(solution)/shard_map/all_gather | solution.py:49
  163.3 33.3 %collective-permute-start = (f32[1328]{0:T(1024)S(1)}, f32[1328]{0:T(1024)S(1)}, u32[]{:S(2)}, u32[]{:S(2)}) collective-permute-start(f32[1328]{0:T(1024)S(1)} %copy-done.11), channel_id=1, source_target_pairs={{0,2},{2,4},{4,6},{6,8},{8,10},{10,12},{12,14},{14,16},{16,18},{18... | collective-permute-start | bytes 15944 | tf_op jit(solution)/shard_map/ppermute | solution.py:15
  166.7 29.9 %collective-permute-start.1 = (f32[1328]{0:T(1024)S(1)}, f32[1328]{0:T(1024)S(1)}, u32[]{:S(2)}, u32[]{:S(2)}) collective-permute-start(f32[1328]{0:T(1024)S(1)} %copy-done.11), channel_id=1, source_target_pairs={{2,0},{4,2},{6,4},{8,6},{10,8},{12,10},{14,12},{16,14},{18,16},{20... | collective-permute-start | bytes 15944 | tf_op jit(solution)/shard_map/ppermute | solution.py:18
  171.0 43.2 %copy-start.8 = (s32[3072]{0:T(1024)}, s32[3072]{0:T(1024)S(1)}, u32[]{:S(2)}) copy-start(s32[3072]{0:T(1024)S(1)} %get-tuple-element.19) | copy-start | bytes 36868
  187.6 9.1 %copy-start.3 = (f32[3984]{0:T(1024)}, f32[3984]{0:T(1024)S(1)}, u32[]{:S(2)}) copy-start(f32[3984]{0:T(1024)S(1)} %scatter_custom_fusion.1) | copy-start | bytes 47812
  188.3 473.5 %collective-permute-start.4 = (f32[1328]{0:T(1024)}, f32[1328]{0:T(1024)}, u32[]{:S(2)}, u32[]{:S(2)}) collective-permute-start(f32[1328]{0:T(1024)} %get-tuple-element.44), channel_id=1, source_target_pairs={{2,0},{4,2},{6,4},{8,6},{10,8},{12,10},{14,12},{16,14},{18,16},{20... | collective-permute-start | bytes 15944 | tf_op jit(solution)/shard_map/ppermute | solution.py:26
  190.9 470.9 %collective-permute-start.5 = (f32[1328]{0:T(1024)}, f32[1328]{0:T(1024)}, u32[]{:S(2)}, u32[]{:S(2)}) collective-permute-start(f32[1328]{0:T(1024)} %get-tuple-element.45), channel_id=1, source_target_pairs={{0,2},{2,4},{4,6},{6,8},{8,10},{10,12},{12,14},{14,16},{16,18},{18... | collective-permute-start | bytes 15944 | tf_op jit(solution)/shard_map/ppermute | solution.py:26
  196.7 17.5 %copy-start.6 = (s32[3072]{0:T(1024)S(1)}, s32[3072]{0:T(1024)}, u32[]{:S(2)}) copy-start(s32[3072]{0:T(1024)} %param.9) | copy-start | bytes 36868
  196.7 17.5 %copy-start = (bf16[3072,512]{1,0:T(8,128)(2,1)S(1)}, bf16[3072,512]{1,0:T(8,128)(2,1)}, u32[]{:S(2)}) copy-start(bf16[3072,512]{1,0:T(8,128)(2,1)} %param.7) | copy-start | bytes 9437188
  270.9 1.9 copy-start.1
  301.4 0.8 copy-start.2
  414.6 66.7 %copy-start.14 = (f32[128]{0:T(128)S(1)}, f32[128]{0:T(128)}, u32[]{:S(2)}) copy-start(f32[128]{0:T(128)} %get-tuple-element.42) | copy-start | bytes 1540
  414.6 66.7 %copy-start.15 = (f32[128]{0:T(128)S(1)}, f32[128]{0:T(128)}, u32[]{:S(2)}) copy-start(f32[128]{0:T(128)} %get-tuple-element.39) | copy-start | bytes 1540
  486.9 4.8 copy-start.17
  486.9 130.4 %copy-start.9 = (f32[2,1,512]{2,1,0:T(1,128)S(1)}, f32[2,1,512]{2,1,0:T(1,128)}, u32[]{:S(2)}) copy-start(f32[2,1,512]{2,1,0:T(1,128)} %all-gather.1) | copy-start | bytes 12292
  519.9 118.9 %copy-start.7 = (s32[3072]{0:T(1024)S(1)}, s32[3072]{0:T(1024)}, u32[]{:S(2)}) copy-start(s32[3072]{0:T(1024)} %param.9) | copy-start | bytes 36868
  519.9 147.4 %copy-start.4 = (f32[3984]{0:T(1024)S(1)}, f32[3984]{0:T(1024)}, u32[]{:S(2)}) copy-start(f32[3984]{0:T(1024)} %copy-done.3) | copy-start | bytes 47812
  519.9 147.4 %copy-start.12 = (f32[1328]{0:T(1024)S(1)}, f32[1328]{0:T(1024)}, u32[]{:S(2)}) copy-start(f32[1328]{0:T(1024)} %param.13) | copy-start | bytes 15940
  634.5 34.1 %copy-start.13 = (f32[512,1]{0,1:T(1,128)}, f32[512,1]{0,1:T(1,128)S(1)}, u32[]{:S(2)}) copy-start(f32[512,1]{0,1:T(1,128)S(1)} %constant_dynamic-slice_fusion.1) | copy-start | bytes 6148
  655.6 6.2 collective-permute-start.2
  659.9 7.3 %collective-permute-start.3 = (f32[1328]{0:T(1024)S(1)}, f32[1328]{0:T(1024)S(1)}, u32[]{:S(2)}, u32[]{:S(2)}) collective-permute-start(f32[1328]{0:T(1024)S(1)} %get-tuple-element.47), channel_id=1, source_target_pairs={{0,2},{2,4},{4,6},{6,8},{8,10},{10,12},{12,14},{14,16},{16,18},{18... | collective-permute-start | bytes 15944 | tf_op jit(solution)/shard_map/ppermute | solution.py:26
Sparse Core Ops, SparseCore 0:
  9.5 18.1 all-gather.4
  36.5 126.6 all-reduce.2
  164.9 13.4 all-gather.6
where the time goes:
time: 687 us; the launch traced here: 675 us
  other arithmetic  311 us (45%)
  waiting for transfers between devices  153 us (22%)
  matrix products  69.7 us (10%)
  local copies, waits for them, and re-layouts  63.9 us (9%)
  blocking collectives  38.9 us (6%)
  starting transfers between devices  19.8 us (3%)
  between operations  19.4 us (3%)
    another operation x30, other arithmetic, local(): lower = jnp.linalg.cholesky(precision)  179 us
    psum x1, waiting for transfers between devices, local(): gram_block, rhs_block = lax.psum((gram_block, rhs_block), 'rows')  127 us
    another operation x3, other arithmetic, local(): beta = jax.scipy.linalg.solve_triangular(lower, inner, trans=1, lower=True)  85.6 us
    psum x1, blocking collectives, local(): gram_block, rhs_block = lax.psum((gram_block, rhs_block), 'rows')  31.9 us
    another operation x24, local copies, waits for them, and re-layouts  28.1 us
    another operation x14, matrix products, local(): lower = jnp.linalg.cholesky(precision)  25.7 us
    all_gather x1, waiting for transfers between devices, local(): lax.all_gather(design, 'cov', axis=1, tiled=True)  19.8 us
    gather x1, local copies, waits for them, and re-layouts, local(): effect_row = jnp.take(window, local_id)  17.4 us
  transfers between devices with their start and end apart: 9, of which 3 were waited for; matrix products, arithmetic and copies ran while one was open for 64% of the time, Pallas kernels for 0%

commit v1 on v0

--- a/solution.py
+++ b/solution.py
@@ -5,6 +5,8 @@
 
 prior_precision = 1.0
 tract_precision = 1.0
+BLOCK = 128
+HIGH = lax.Precision.HIGHEST
 
 
 def extended(block, sides, width):
@@ -32,6 +34,47 @@
     )
 
 
+def mm(a, b):
+    return jnp.dot(a, b, precision=HIGH, preferred_element_type=jnp.float32)
+
+
+def factor(precision):
+    order = precision.shape[0]
+    eye = jnp.eye(BLOCK, dtype=jnp.float32)
+    trailing = precision
+    inverses, panels = [], []
+    for k in range(order // BLOCK):
+        diag = lax.linalg.cholesky(trailing[:BLOCK, :BLOCK], symmetrize_input=False)
+        inverse = lax.linalg.triangular_solve(diag, eye, left_side=True, lower=True)
+        inverses.append(inverse)
+        if trailing.shape[0] > BLOCK:
+            panel = mm(trailing[BLOCK:, :BLOCK], inverse.T)
+            panels.append(panel)
+            trailing = trailing[BLOCK:, BLOCK:] - mm(panel, panel.T)
+    return inverses, panels
+
+
+def draw(inverses, panels, rhs, noise):
+    count = len(inverses)
+    rest = rhs
+    inner = []
+    for k in range(count):
+        part = mm(inverses[k], rest[:BLOCK])
+        inner.append(part + noise[k * BLOCK : (k + 1) * BLOCK])
+        if k < count - 1:
+            rest = rest[BLOCK:] - mm(panels[k], part)
+    solved = []
+    below = None
+    for k in reversed(range(count)):
+        value = inner[k]
+        if below is not None:
+            value = value - mm(panels[k].T, below)
+        part = mm(inverses[k].T, value)
+        solved.insert(0, part)
+        below = part if below is None else jnp.concatenate([part, below])
+    return jnp.concatenate(solved)
+
+
 def local(design, tract_id, outcome, omega, effects_old, normal_coef, normal_tract):
     columns = design.shape[1]
     tract_dev = effects_old.shape[0]
@@ -43,18 +86,16 @@
     offset = lax.axis_index("cov") * columns
     weighted = (omega[:, None] * design).astype(jnp.bfloat16)
     gram_block = contract_rows(lax.all_gather(design, "cov", axis=1, tiled=True), weighted)
-    rhs_block = contract_rows(design, resid)
-    gram_block, rhs_block = lax.psum((gram_block, rhs_block), "rows")
-    gram, rhs, noise = (
-        lax.all_gather(gram_block, "cov", axis=1, tiled=True),
-        lax.all_gather(rhs_block, "cov", axis=0, tiled=True),
-        lax.all_gather(normal_coef, "cov", axis=0, tiled=True),
-    )
-    order = gram.shape[0]
+    rhs_block = contract_rows(resid, design)
+    pad = jnp.zeros((7, columns), jnp.float32)
+    stacked = jnp.concatenate([gram_block, rhs_block[None, :], normal_coef[None, :], pad])
+    order = gram_block.shape[0]
+    summed = jnp.concatenate([lax.psum(stacked[: order + 1], "rows"), stacked[order + 1 :]])
+    full = lax.all_gather(summed, "cov", axis=1, tiled=True)
+    gram, rhs, noise = full[:order], full[order], full[order + 1]
     precision = 0.5 * (gram + gram.T) + prior_precision * jnp.eye(order, dtype=jnp.float32)
-    lower = jnp.linalg.cholesky(precision)
-    inner = jax.scipy.linalg.solve_triangular(lower, rhs, lower=True) + noise
-    beta = jax.scipy.linalg.solve_triangular(lower, inner, trans=1, lower=True)
+    inverses, panels = factor(precision)
+    beta = draw(inverses, panels, rhs, noise)
     beta_b = beta.astype(jnp.bfloat16)
     beta_own = lax.dynamic_slice_in_dim(beta, offset, columns)
     own_coef = lax.dynamic_slice_in_dim(beta_b, offset, columns)

time: 687 us -> 600 us (0.87)
  other arithmetic: 311 us -> 265 us
  blocking collectives: 38.9 us -> 3.3 us
  waiting for transfers between devices: 153 us -> 139 us
  local copies, waits for them, and re-layouts: 63.9 us -> 75.7 us
    dot_general x0 -> x44, matrix products: none -> 54 us  [mm(): return jnp.dot(a, b, precision=HIGH, preferred_element_type=jnp.float32)]
    another operation x44 -> x8, matrix products: 59.7 us -> 7.3 us  [factor(): inverse = lax.linalg.triangular_solve(diag, eye, left_side=True, lower=True)]
    another operation x33 -> x40, other arithmetic: 265 us -> 215 us  [the longest x24 114 us: factor(): diag = lax.linalg.cholesky(trailing[:BLOCK, :BLOCK], symmetrize_input=False)]
    psum x1 -> x0, blocking collectives: 31.9 us -> none  [local(): gram_block, rhs_block = lax.psum((gram_block, rhs_block), 'rows')]
    another operation x37 -> x0, local copies, waits for them, and re-layouts: 31.3 us -> none
    unnamed x54 -> x102, local copies, waits for them, and re-layouts: 3.09 us -> 32.6 us
    all_gather x1, waiting for transfers between devices: 19.8 us -> 0.02 us  [local(): lax.all_gather(design, 'cov', axis=1, tiled=True)]
    slice x0 -> x11, local copies, waits for them, and re-layouts: none -> 16.8 us  [the longest x2 10.3 us: local(): gram, rhs, noise = (full[:order], full[order], full[order + 1])]
  transfers between devices with their start and end apart: 9 -> 9, of which waited for: 3 -> 3; matrix products, arithmetic and copies ran while one was open for 64% -> 67% of each run, Pallas kernels for 0% -> 0%
where the time goes in v1:
time: 600 us; the launch traced here: 590 us
  other arithmetic  265 us (44%)
  waiting for transfers between devices  139 us (23%)
  local copies, waits for them, and re-layouts  75.7 us (13%)
  matrix products  69.9 us (12%)
  starting transfers between devices  21.7 us (4%)
  between operations  15.1 us (3%)
    psum x1, waiting for transfers between devices, local(): lax.psum(stacked[:order + 1], 'rows')  133 us
    another operation x24, other arithmetic, factor(): diag = lax.linalg.cholesky(trailing[:BLOCK, :BLOCK], symmetrize_input=False)  114 us
    another operation x16, other arithmetic, factor(): inverse = lax.linalg.triangular_solve(diag, eye, left_side=True, lower=True)  101 us
    dot_general x44, matrix products, mm(): return jnp.dot(a, b, precision=HIGH, preferred_element_type=jnp.float32)  54 us
    unnamed x102, local copies, waits for them, and re-layouts  32.6 us
    gather x1, local copies, waits for them, and re-layouts, local(): effect_row = jnp.take(window, local_id)  17.4 us
    scatter-add x1, other arithmetic, local(): jax.ops.segment_sum(contrib, local_id, num_segments=3 * tract_dev)  16.7 us
    scatter-add x1, other arithmetic, local(): jax.ops.segment_sum(omega, local_id, num_segments=3 * tract_dev)  16.6 us
  transfers between devices with their start and end apart: 9, of which 3 were waited for; matrix products, arithmetic and copies ran while one was open for 67% of the time, Pallas kernels for 0%

profile of v1, /device:TPU:8, one launch (start us, length us, event | category | flops | bytes accessed | tf_op | source)
XLA Modules:
  0.0 589.9 jit_solution(5513657509580126814)
XLA Ops:
  8.0 3.4 collective-permute-start
  11.4 4.2 collective-permute-start.1
  17.1 17.4 %gather_fusion = f32[3072]{0:T(1024)S(1)} fusion(f32[3984]{0:T(1024)S(1)} %concatenate.39, s32[3072]{0:T(1024)S(1)} %get-tuple-element.13), kind=kCustom, calls=%fused_computation | custom fusion | bytes 36864 | tf_op jit(solution)/shard_map/jit(_take)/gather | solution.py:84
  35.9 6.3 %fusion.4 = f32[1024,512]{0,1:T(8,128)S(1)} fusion(bf16[3072,1024]{1,0:T(8,128)(2,1)} %all-gather.3.cloned.1.call-done, bf16[3072,512]{1,0:T(8,128)(2,1)S(1)} %copy-done, f32[3072]{0:T(1024)S(1)} %copy-done.21), kind=kOutput, calls=%fused_computation.16 | convolution fusion | flops 3225944064 | bytes 11546624 | tf_op jit(solution)/shard_map/dot_general | solution.py:32
  44.1 132.7 %all-reduce.3.cloned.1.call-done = f32[1025,512]{0,1:T(8,128)} async-done(((f32[1025,512]{0,1:T(8,128)}), f32[1025,512]{0,1:T(8,128)}) %all-reduce.3.cloned.1.call-update) | async-done | bytes 2099216 | tf_op jit(solution)/shard_map/psum | solution.py:93
  176.7 3.3 select_maximum_fusion
  180.1 16.6 %scatter_custom_fusion.1 = f32[3984]{0:T(1024)S(1)} fusion(s32[3072]{0:T(1024)S(1)} %get-tuple-element.14, f32[3072]{0:T(1024)S(1)} %copy-done.21, f32[]{:T(128)} %constant.56.clone.1), kind=kCustom, calls=%fused_computation.184 | custom fusion | flops 3072 | bytes 15940 | tf_op jit(solution)/shard_map/scatter-add | solution.py:105
  197.3 4.4 collective-permute-start.4
  201.7 1.9 collective-permute-start.5
  203.7 4.8 slice.262
  208.5 5.5 copy.12
  214.0 4.5 fusion.1
  218.5 2.0 copy-done.1
  220.5 11.7 %custom-call.20 = f32[128,128]{1,0:T(8,128)S(1)} custom-call(f32[128,128]{1,0:T(8,128)S(1)} %slice.263), custom_call_target="Cholesky" | custom-call | tf_op jit(solution)/shard_map/cholesky/custom-call.1 | solution.py:47
  233.6 9.8 %custom-call.21 = f32[1,128,128]{1,2,0:T(8,128)S(1)} custom-call(f32[1,128,128]{2,1,0:T(8,128)S(1)} %fusion.57), custom_call_target="InvertDiagBlocksLowerTriangular" | custom-call | tf_op jit(solution)/shard_map/triangular_solve/custom-call.0 | solution.py:48
  245.3 5.0 slice_subtract_fusion
  250.3 1.7 copy-done.3
  252.0 11.9 %custom-call.22 = f32[128,128]{1,0:T(8,128)S(1)} custom-call(f32[128,128]{1,0:T(8,128)S(1)} %slice.268), custom_call_target="Cholesky" | custom-call | tf_op jit(solution)/shard_map/cholesky/custom-call.1 | solution.py:47
  265.2 9.8 %custom-call.23 = f32[1,128,128]{1,2,0:T(8,128)S(1)} custom-call(f32[1,128,128]{2,1,0:T(8,128)S(1)} %fusion.58), custom_call_target="InvertDiagBlocksLowerTriangular" | custom-call | tf_op jit(solution)/shard_map/triangular_solve/custom-call.0 | solution.py:48
  275.3 2.1 slice_reduce_fusion.8
  282.8 3.7 slice_subtract_fusion.1
  288.5 13.6 %custom-call.24 = f32[128,128]{1,0:T(8,128)} custom-call(f32[128,128]{1,0:T(8,128)} %slice.273), custom_call_target="Cholesky" | custom-call | tf_op jit(solution)/shard_map/cholesky/custom-call.1 | solution.py:47
  303.6 2.1 fusion.59
  305.7 11.3 %custom-call.25 = f32[1,128,128]{1,2,0:T(8,128)} custom-call(f32[1,128,128]{2,1,0:T(8,128)} %fusion.59), custom_call_target="InvertDiagBlocksLowerTriangular" | custom-call | tf_op jit(solution)/shard_map/triangular_solve/custom-call.0 | solution.py:48
  320.4 2.9 slice_subtract_fusion.2
  325.2 13.2 %custom-call.26 = f32[128,128]{1,0:T(8,128)} custom-call(f32[128,128]{1,0:T(8,128)} %slice.277), custom_call_target="Cholesky" | custom-call | tf_op jit(solution)/shard_map/cholesky/custom-call.1 | solution.py:47
  339.9 2.1 fusion.60
  342.0 11.3 %custom-call.27 = f32[1,128,128]{1,2,0:T(8,128)} custom-call(f32[1,128,128]{2,1,0:T(8,128)} %fusion.60), custom_call_target="InvertDiagBlocksLowerTriangular" | custom-call | tf_op jit(solution)/shard_map/triangular_solve/custom-call.0 | solution.py:48
  356.6 2.5 convolution_subtract_fusion
  360.7 13.2 %custom-call.28 = f32[128,128]{1,0:T(8,128)} custom-call(f32[128,128]{1,0:T(8,128)} %slice.281), custom_call_target="Cholesky" | custom-call | tf_op jit(solution)/shard_map/cholesky/custom-call.1 | solution.py:47
  375.5 2.1 fusion.61
  377.6 11.3 %custom-call.29 = f32[1,128,128]{1,2,0:T(8,128)} custom-call(f32[1,128,128]{2,1,0:T(8,128)} %fusion.61), custom_call_target="InvertDiagBlocksLowerTriangular" | custom-call | tf_op jit(solution)/shard_map/triangular_solve/custom-call.0 | solution.py:48
  392.2 1.8 convolution_subtract_fusion.1
  396.2 13.2 %custom-call.30 = f32[128,128]{1,0:T(8,128)} custom-call(f32[128,128]{1,0:T(8,128)} %slice.285), custom_call_target="Cholesky" | custom-call | tf_op jit(solution)/shard_map/cholesky/custom-call.1 | solution.py:47
  411.1 2.1 fusion.62
  413.2 11.3 %custom-call.31 = f32[1,128,128]{1,2,0:T(8,128)} custom-call(f32[1,128,128]{2,1,0:T(8,128)} %fusion.62), custom_call_target="InvertDiagBlocksLowerTriangular" | custom-call | tf_op jit(solution)/shard_map/triangular_solve/custom-call.0 | solution.py:48
  431.2 13.2 %custom-call.32 = f32[128,128]{1,0:T(8,128)} custom-call(f32[128,128]{1,0:T(8,128)} %slice.289), custom_call_target="Cholesky" | custom-call | tf_op jit(solution)/shard_map/cholesky/custom-call.1 | solution.py:47
  445.9 2.1 fusion.63
  448.0 11.3 %custom-call.33 = f32[1,128,128]{1,2,0:T(8,128)} custom-call(f32[1,128,128]{2,1,0:T(8,128)} %fusion.63), custom_call_target="InvertDiagBlocksLowerTriangular" | custom-call | tf_op jit(solution)/shard_map/triangular_solve/custom-call.0 | solution.py:48
  462.4 1.8 convolution_subtract_fusion.3
  465.7 13.4 %custom-call.34 = f32[128,128]{1,0:T(8,128)} custom-call(f32[128,128]{1,0:T(8,128)} %convolution_subtract_fusion.3), custom_call_target="Cholesky" | custom-call | tf_op jit(solution)/shard_map/cholesky/custom-call.1 | solution.py:47
  480.6 2.1 fusion.64
  482.8 11.3 %custom-call.35 = f32[1,128,128]{1,2,0:T(8,128)} custom-call(f32[1,128,128]{2,1,0:T(8,128)} %fusion.64), custom_call_target="InvertDiagBlocksLowerTriangular" | custom-call | tf_op jit(solution)/shard_map/triangular_solve/custom-call.0 | solution.py:48
  548.3 3.3 psum.15
  551.7 16.7 %scatter_custom_fusion = f32[3984]{0:T(1024)S(1)} fusion(s32[3072]{0:T(1024)} %copy-done.25, f32[3072]{0:T(1024)S(1)} %multiply_subtract_fusion, f32[]{:T(128)} %constant.56.clone.1), kind=kCustom, calls=%fused_computation.186 | custom fusion | flops 3072 | bytes 16448 | tf_op jit(solution)/shard_map/scatter-add | solution.py:106
  568.5 5.7 collective-permute-start.2
  574.2 1.9 collective-permute-start.3
  576.8 4.7 collective-permute-done.3
  (222 shorter events, 110.8 us)
Async XLA Ops:
  7.2 0.8 copy-start.30
  7.2 8.5 %copy-start.28 = (s32[3072]{0:T(1024)S(1)}, s32[3072]{0:T(1024)}, u32[]{:S(2)}) copy-start(s32[3072]{0:T(1024)} %param.11) | copy-start | bytes 36868
  7.2 28.7 %all-gather.3.cloned.1.call-start = ((), (), s32[]{:S(2)}) async-start(), calls=%async_computation | async-start | bytes 9437184 | tf_op jit(solution)/shard_map/all_gather | solution.py:88
  7.9 168.8 %all-reduce.3.cloned.1.call-start = ((), (), s32[]{:S(2)}) async-start(), calls=%async_computation.1 | async-start | bytes 4718592 | tf_op jit(solution)/shard_map/psum | solution.py:93
  8.0 7.7 %collective-permute-start = (f32[1328]{0:T(1024)S(1)}, f32[1328]{0:T(1024)S(1)}, u32[]{:S(2)}, u32[]{:S(2)}) collective-permute-start(f32[1328]{0:T(1024)S(1)} %copy-done.30), channel_id=1, source_target_pairs={{0,2},{2,4},{4,6},{6,8},{8,10},{10,12},{12,14},{14,16},{16,18},{18... | collective-permute-start | bytes 15944 | tf_op jit(solution)/shard_map/ppermute | solution.py:17
  11.4 5.6 collective-permute-start.1
  15.7 164.4 %copy-start.25 = (s32[3072]{0:T(1024)}, s32[3072]{0:T(1024)S(1)}, u32[]{:S(2)}) copy-start(s32[3072]{0:T(1024)S(1)} %get-tuple-element.14) | copy-start | bytes 36868
  17.1 17.4 %copy-start.21 = (f32[3072]{0:T(1024)S(1)}, f32[3072]{0:T(1024)}, u32[]{:S(2)}) copy-start(f32[3072]{0:T(1024)} %param.13) | copy-start | bytes 36868
  17.1 17.5 %copy-start.23 = (s32[3072]{0:T(1024)S(1)}, s32[3072]{0:T(1024)}, u32[]{:S(2)}) copy-start(s32[3072]{0:T(1024)} %param.12) | copy-start | bytes 36868
  17.1 17.5 %copy-start = (bf16[3072,512]{1,0:T(8,128)(2,1)S(1)}, bf16[3072,512]{1,0:T(8,128)(2,1)}, u32[]{:S(2)}) copy-start(bf16[3072,512]{1,0:T(8,128)(2,1)} %param.10) | copy-start | bytes 9437188
  42.2 1.7 copy-start.39
  43.9 159.9 %all-gather.5.cloned.1.call-start = ((), (), s32[]{:S(2)}) async-start(), calls=%async_computation.2 | async-start | bytes 7077888 | tf_op jit(solution)/shard_map/all_gather | solution.py:94
  197.3 379.4 %collective-permute-start.4 = (f32[1328]{0:T(1024)}, f32[1328]{0:T(1024)}, u32[]{:S(2)}, u32[]{:S(2)}) collective-permute-start(f32[1328]{0:T(1024)} %get-tuple-element.15), channel_id=1, source_target_pairs={{2,0},{4,2},{6,4},{8,6},{10,8},{12,10},{14,12},{16,14},{18,16},{20... | collective-permute-start | bytes 15944 | tf_op jit(solution)/shard_map/ppermute | solution.py:28
  201.7 375.1 %collective-permute-start.5 = (f32[1328]{0:T(1024)}, f32[1328]{0:T(1024)}, u32[]{:S(2)}, u32[]{:S(2)}) collective-permute-start(f32[1328]{0:T(1024)} %get-tuple-element.16), channel_id=1, source_target_pairs={{0,2},{2,4},{4,6},{6,8},{8,10},{10,12},{12,14},{14,16},{16,18},{18... | collective-permute-start | bytes 15944 | tf_op jit(solution)/shard_map/ppermute | solution.py:28
  218.5 2.0 copy-start.1
  243.7 33.8 %copy-start.19 = (f32[128,128]{1,0:T(8,128)}, f32[128,128]{1,0:T(8,128)S(1)}, u32[]{:S(2)}) copy-start(f32[128,128]{1,0:T(8,128)S(1)} %fusion.49) | copy-start | bytes 196612
  245.3 5.0 copy-start.2
  250.3 1.7 copy-start.3
  275.3 7.3 %copy-start.17 = (f32[128,128]{1,0:T(8,128)}, f32[128,128]{1,0:T(8,128)S(1)}, u32[]{:S(2)}) copy-start(f32[128,128]{1,0:T(8,128)S(1)} %fusion.47) | copy-start | bytes 196612
  282.8 5.1 copy-start.32
  286.5 1.4 copy-start.5
  317.0 6.8 %copy-start.26 = (f32[768]{0:T(1024)S(1)}, f32[768]{0:T(1024)}, u32[]{:S(2)}) copy-start(f32[768]{0:T(1024)} %slice_subtract_fusion.4) | copy-start | bytes 9220
  318.1 1.4 copy-start.18
  319.6 3.8 copy-start.4
  320.4 4.1 copy-start.33
  323.4 1.2 copy-start.7
  353.2 6.2 %copy-start.27 = (f32[640]{0:T(1024)S(1)}, f32[640]{0:T(1024)}, u32[]{:S(2)}) copy-start(f32[640]{0:T(1024)} %slice_subtract_fusion.3) | copy-start | bytes 7684
  354.4 1.4 copy-start.13
  355.8 3.4 copy-start.6
  356.6 3.4 copy-start.34
  359.1 1.0 copy-start.9
  390.0 1.3 copy-start.14
  391.3 2.7 copy-start.8
  392.2 3.4 copy-start.35
  393.9 1.6 copy-start.11
  425.6 3.7 copy-start.15
  426.8 2.3 copy-start.10
  427.7 1.6 copy-start.36
  429.1 1.5 copy-start.20
  460.4 1.1 copy-start.16
  461.6 2.7 copy-start.12
  462.4 1.8 copy-start.37
  523.3 28.3 %copy-start.22 = (f32[3072]{0:T(1024)S(1)}, f32[3072]{0:T(1024)}, u32[]{:S(2)}) copy-start(f32[3072]{0:T(1024)} %param.13) | copy-start | bytes 36868
  523.3 28.3 %copy-start.24 = (s32[3072]{0:T(1024)S(1)}, s32[3072]{0:T(1024)}, u32[]{:S(2)}) copy-start(s32[3072]{0:T(1024)} %param.12) | copy-start | bytes 36868
  523.3 58.2 %copy-start.31 = (f32[1328]{0:T(1024)S(1)}, f32[1328]{0:T(1024)}, u32[]{:S(2)}) copy-start(f32[1328]{0:T(1024)} %param.16) | copy-start | bytes 15940
  546.6 29.5 %copy-start.29 = (f32[1024]{0:T(1024)S(1)}, f32[1024]{0:T(1024)}, u32[]{:S(2)}) copy-start(f32[1024]{0:T(1024)} %constant_dynamic-update-slice_fusion.25) | copy-start | bytes 12292
  568.5 8.3 %collective-permute-start.2 = (f32[1328]{0:T(1024)S(1)}, f32[1328]{0:T(1024)S(1)}, u32[]{:S(2)}, u32[]{:S(2)}) collective-permute-start(f32[1328]{0:T(1024)S(1)} %get-tuple-element.17), channel_id=1, source_target_pairs={{2,0},{4,2},{6,4},{8,6},{10,8},{12,10},{14,12},{16,14},{18,16},{20... | collective-permute-start | bytes 15944 | tf_op jit(solution)/shard_map/ppermute | solution.py:28
  574.2 7.3 %collective-permute-start.3 = (f32[1328]{0:T(1024)S(1)}, f32[1328]{0:T(1024)S(1)}, u32[]{:S(2)}, u32[]{:S(2)}) collective-permute-start(f32[1328]{0:T(1024)S(1)} %get-tuple-element.18), channel_id=1, source_target_pairs={{0,2},{2,4},{4,6},{6,8},{8,10},{10,12},{12,14},{14,16},{16,18},{18... | collective-permute-start | bytes 15944 | tf_op jit(solution)/shard_map/ppermute | solution.py:28
  (1 other events, 0.6 us)
Sparse Core Ops, SparseCore 0:
  9.6 18.1 all-gather.2
  44.0 132.7 all-reduce.2
  180.2 14.3 all-gather.4

commit v2 on v0

--- a/solution.py
+++ b/solution.py
@@ -1,10 +1,14 @@
 import jax
 import jax.numpy as jnp
 from jax import lax
+from jax.experimental import pallas as pl
+from jax.experimental.pallas import tpu as pltpu
 from jax.sharding import PartitionSpec as P
 
 prior_precision = 1.0
 tract_precision = 1.0
+BLOCK = 128
+HIGH = lax.Precision.HIGHEST
 
 
 def extended(block, sides, width):
@@ -32,6 +36,117 @@
     )
 
 
+def mm(a, b):
+    return jnp.dot(a, b, precision=HIGH, preferred_element_type=jnp.float32)
+
+
+def inverse_kernel(a_ref, inv_ref, work):
+    size = a_ref.shape[0]
+    work[...] = a_ref[...]
+    rows = lax.broadcasted_iota(jnp.int32, (size, size), 0)
+    lanes = lax.broadcasted_iota(jnp.int32, (size, size), 1)
+    inv_ref[...] = jnp.where(rows == lanes, 1.0, 0.0).astype(jnp.float32)
+    lane = lax.broadcasted_iota(jnp.int32, (1, size), 1)
+    sub = lax.broadcasted_iota(jnp.int32, (size, 1), 0)
+
+    def step(k, carry):
+        row = work[pl.ds(k, 1), :]
+        pivot = jnp.sum(jnp.where(lane == k, row, 0.0), axis=1, keepdims=True)
+        scale = lax.rsqrt(pivot)
+        whole = work[...]
+        column = jnp.sum(jnp.where(lanes == k, whole, 0.0), axis=1, keepdims=True)
+        below = jnp.where(sub > k, column * scale, 0.0)
+        tail = jnp.where(lane > k, row * scale, 0.0)
+        work[...] = whole - below * tail
+        lead = inv_ref[pl.ds(k, 1), :] * scale
+        current = inv_ref[...]
+        inv_ref[...] = jnp.where(rows == k, lead, current - below * lead)
+        return carry
+
+    lax.fori_loop(0, size, step, 0)
+
+
+def block_inverse(block):
+    size = block.shape[0]
+    return pl.pallas_call(
+        inverse_kernel,
+        out_shape=jax.ShapeDtypeStruct((size, size), jnp.float32),
+        in_specs=[pl.BlockSpec(memory_space=pltpu.VMEM)],
+        out_specs=pl.BlockSpec(memory_space=pltpu.VMEM),
+        scratch_shapes=[pltpu.VMEM((size, size), jnp.float32)],
+        cost_estimate=pl.CostEstimate(flops=4 * size ** 3, bytes_accessed=8 * size * size, transcendentals=size),
+    )(block)
+
+
+def factor(precision, rhs):
+    order = precision.shape[0]
+    extra = jnp.zeros((8, order), jnp.float32).at[0].set(rhs)
+    trailing = jnp.concatenate([precision, extra])
+    inverses, panels, forward = [], [], []
+    for k in range(order // BLOCK):
+        inverse = block_inverse(trailing[:BLOCK, :BLOCK])
+        inverses.append(inverse)
+        full = mm(trailing[BLOCK:, :BLOCK], inverse.T)
+        forward.append(full[-8])
+        panel = full[:-8]
+        if panel.shape[0]:
+            panels.append(panel)
+            trailing = trailing[BLOCK:, BLOCK:] - mm(full, panel.T)
+    return inverses, panels, forward
+
+
+def backward(inverses, panels, forward, noise):
+    count = len(inverses)
+    solved = []
+    below = None
+    for k in reversed(range(count)):
+        value = forward[k] + noise[k * BLOCK : (k + 1) * BLOCK]
+        if below is not None:
+            value = value - mm(panels[k].T, below)
+        part = mm(inverses[k].T, value)
+        solved.insert(0, part)
+        below = part if below is None else jnp.concatenate([part, below])
+    return jnp.concatenate(solved)
+
+
+def pair_gather(block, axis, dim):
+    if lax.axis_size(axis) != 2:
+        return lax.all_gather(block, axis, axis=dim, tiled=True)
+    other = lax.ppermute(block, axis, [(0, 1), (1, 0)])
+    first = lax.axis_index(axis) == 0
+    return jnp.concatenate(
+        [jnp.where(first, block, other), jnp.where(first, other, block)], axis=dim
+    )
+
+
+def pair_sum(block, axis):
+    if lax.axis_size(axis) != 2:
+        return lax.psum(block, axis)
+    return block + lax.ppermute(block, axis, [(0, 1), (1, 0)])
+
+
+def halving_sum(data, axis, late):
+    count = lax.axis_size(axis)
+    index = lax.axis_index(axis)
+    bits = [1 << b for b in range(count.bit_length() - 1)]
+    for bit in bits:
+        route = [(i, i ^ bit) for i in range(count)]
+        half = data.shape[0] // 2
+        upper = (index & bit) != 0
+        send = jnp.where(upper, data[:half], data[half:])
+        keep = jnp.where(upper, data[half:], data[:half])
+        data = keep + lax.ppermute(send, axis, route)
+    data = jnp.concatenate([data, late])
+    for bit in reversed(bits):
+        route = [(i, i ^ bit) for i in range(count)]
+        upper = (index & bit) != 0
+        other = lax.ppermute(data, axis, route)
+        data = jnp.concatenate(
+            [jnp.where(upper, other, data), jnp.where(upper, data, other)]
+        )
+    return data.reshape(count, -1, data.shape[-1])
+
+
 def local(design, tract_id, outcome, omega, effects_old, normal_coef, normal_tract):
     columns = design.shape[1]
     tract_dev = effects_old.shape[0]
@@ -40,28 +155,58 @@
     local_id = tract_id - (lax.axis_index("rows") - 1) * tract_dev
     effect_row = jnp.take(window, local_id)
     resid = (kappa - omega * effect_row).astype(jnp.bfloat16)
-    offset = lax.axis_index("cov") * columns
+    core = lax.axis_index("cov")
+    offset = core * columns
+    half = columns // 2
     weighted = (omega[:, None] * design).astype(jnp.bfloat16)
-    gram_block = contract_rows(lax.all_gather(design, "cov", axis=1, tiled=True), weighted)
-    rhs_block = contract_rows(design, resid)
-    gram_block, rhs_block = lax.psum((gram_block, rhs_block), "rows")
-    gram, rhs, noise = (
-        lax.all_gather(gram_block, "cov", axis=1, tiled=True),
-        lax.all_gather(rhs_block, "cov", axis=0, tiled=True),
-        lax.all_gather(normal_coef, "cov", axis=0, tiled=True),
-    )
-    order = gram.shape[0]
-    precision = 0.5 * (gram + gram.T) + prior_precision * jnp.eye(order, dtype=jnp.float32)
-    lower = jnp.linalg.cholesky(precision)
-    inner = jax.scipy.linalg.solve_triangular(lower, rhs, lower=True) + noise
-    beta = jax.scipy.linalg.solve_triangular(lower, inner, trans=1, lower=True)
+    whole = pair_gather(design, "cov", 1)
+    whole_w = (omega[:, None] * whole).astype(jnp.bfloat16)
+    own_gram = contract_rows(design, weighted)
+    own_sym = own_gram + own_gram.T
+    first, second = whole[:, :columns], whole[:, columns:]
+    first_w, second_w = whole_w[:, :columns], whole_w[:, columns:]
+    cols = lax.dynamic_slice_in_dim(first, core * half, half, axis=1)
+    cols_w = lax.dynamic_slice_in_dim(first_w, core * half, half, axis=1)
+    cross = contract_rows(second, cols_w) + contract_rows(cols, second_w).T
+    rhs_block = contract_rows(resid, design)
+    weight_sums = jax.ops.segment_sum(omega, local_id, num_segments=3 * tract_dev)
+    packed = jnp.concatenate([own_sym, cross], axis=1).reshape(-1, BLOCK)
+    packed_rows = packed.shape[0]
+    extra = columns // BLOCK
+    count = lax.axis_size("rows")
+    unit = 8 * count
+    total = -(-packed_rows // unit) * unit
+    if total > packed_rows:
+        packed = jnp.concatenate([packed, jnp.zeros((total - packed_rows, BLOCK), jnp.float32)])
+    late_rows = -(-extra // 8) * 8
+    late = jnp.concatenate(
+        [rhs_block.reshape(-1, BLOCK), jnp.zeros((late_rows - extra, BLOCK), jnp.float32)]
+    ) + 0.0 * weight_sums[0]
+    gathered = halving_sum(packed, "rows", late)
+    chunk = total // count
+    summed = gathered[:, :chunk].reshape(total, BLOCK)
+    rhs_own = jnp.sum(gathered[:, chunk : chunk + extra], axis=0)
+    tail = jnp.concatenate([rhs_own, normal_coef.reshape(-1, BLOCK)])
+    both = pair_gather(jnp.concatenate([summed[:packed_rows], tail])[None], "cov", 0)
+    rhs = both[:, packed_rows : packed_rows + extra].reshape(-1)
+    noise = both[:, packed_rows + extra :].reshape(-1)
+    blocks = both[:, :packed_rows].reshape(2, columns, columns + half)
+    order = 2 * columns
+    sym = jnp.concatenate(
+        [
+            jnp.concatenate([blocks[0, :, :columns], jnp.zeros((columns, columns), jnp.float32)], axis=1),
+            jnp.concatenate([blocks[0, :, columns:], blocks[1, :, columns:], blocks[1, :, :columns]], axis=1),
+        ]
+    )
+    precision = 0.5 * sym + prior_precision * jnp.eye(order, dtype=jnp.float32)
+    inverses, panels, forward = factor(precision, rhs)
+    beta = backward(inverses, panels, forward, noise)
     beta_b = beta.astype(jnp.bfloat16)
     beta_own = lax.dynamic_slice_in_dim(beta, offset, columns)
     own_coef = lax.dynamic_slice_in_dim(beta_b, offset, columns)
     partial_eta = jnp.dot(design, own_coef, preferred_element_type=jnp.float32)
-    eta = lax.psum(partial_eta, "cov")
+    eta = pair_sum(partial_eta, "cov")
     contrib = kappa - omega * eta
-    weight_sums = jax.ops.segment_sum(omega, local_id, num_segments=3 * tract_dev)
     resid_sums = jax.ops.segment_sum(contrib, local_id, num_segments=3 * tract_dev)
     from_above = from_behind((weight_sums[:tract_dev], resid_sums[:tract_dev]), "rows", -1)
     from_below = from_behind((weight_sums[2 * tract_dev :], resid_sums[2 * tract_dev :]), "rows", 1)

time: 687 us -> 416 us (0.61); the launches traced: 675 us -> 413 us
  other arithmetic: 311 us -> 54.2 us
  Pallas kernels: 0 us -> 123 us
  waiting for transfers between devices: 153 us -> 55.7 us
  blocking collectives: 38.9 us -> 0 us
  local copies, waits for them, and re-layouts: 63.9 us -> 90.2 us
  between operations: 19.4 us -> 2.1 us
  matrix products: 69.7 us -> 55.6 us
  starting transfers between devices: 19.8 us -> 32.5 us
    another operation x33 -> x0, other arithmetic: 265 us -> none  [the longest x30 179 us: local(): lower = jnp.linalg.cholesky(precision)]
    psum x1 -> x0, waiting for transfers between devices: 127 us -> none  [local(): gram_block, rhs_block = lax.psum((gram_block, rhs_block), 'rows')]
    pallas_call x0 -> x8, Pallas kernels: none -> 123 us  [block_inverse(): pl.pallas_call(inverse_kernel, out_shape=jax.ShapeDtypeStruct((size, size...]
    another operation x44 -> x0, matrix products: 59.7 us -> none  [the longest x14 25.7 us: local(): lower = jnp.linalg.cholesky(precision)]
    ppermute x0 -> x11, waiting for transfers between devices: none -> 51 us  [the longest x4 29.4 us: halving_sum(): other = lax.ppermute(data, axis, route)]
    dot_general x0 -> x30, matrix products: none -> 46.4 us  [mm(): return jnp.dot(a, b, precision=HIGH, preferred_element_type=jnp.float32)]
    psum x2 -> x0, blocking collectives: 35.2 us -> none  [the longest x1 31.9 us: local(): gram_block, rhs_block = lax.psum((gram_block, rhs_block), 'rows')]
    another operation x37 -> x0, local copies, waits for them, and re-layouts: 31.3 us -> none
  transfers between devices with their start and end apart: 9 -> 17, of which waited for: 3 -> 9; matrix products, arithmetic and copies ran while one was open for 64% -> 20% of each run, Pallas kernels for 0% -> 0%
where the time goes in v2:
time: 416 us; the launch traced here: 413 us
  Pallas kernels  123 us (30%)
  local copies, waits for them, and re-layouts  90.2 us (22%)
  waiting for transfers between devices  55.7 us (13%)
  matrix products  55.6 us (13%)
  other arithmetic  54.2 us (13%)
  starting transfers between devices  32.5 us (8%)
    pallas_call x8, Pallas kernels, block_inverse(): pl.pallas_call(inverse_kernel, out_shape=jax.ShapeDtypeStruct((size, size...  123 us
    dot_general x30, matrix products, mm(): return jnp.dot(a, b, precision=HIGH, preferred_element_type=jnp.float32)  46.4 us
    gather x1, local copies, waits for them, and re-layouts, local(): effect_row = jnp.take(window, local_id)  30.6 us
    ppermute x4, waiting for transfers between devices, halving_sum(): other = lax.ppermute(data, axis, route)  29.4 us
    unnamed x74, local copies, waits for them, and re-layouts  26.3 us
    ppermute x4, waiting for transfers between devices, halving_sum(): data = keep + lax.ppermute(send, axis, route)  17.8 us
    scatter-add x1, other arithmetic, local(): jax.ops.segment_sum(omega, local_id, num_segments=3 * tract_dev)  17.3 us
    scatter-add x1, other arithmetic, local(): jax.ops.segment_sum(contrib, local_id, num_segments=3 * tract_dev)  16.7 us
  transfers between devices with their start and end apart: 17, of which 9 were waited for; matrix products, arithmetic and copies ran while one was open for 20% of the time, Pallas kernels for 0%

profile of v2, /device:TPU:8, one launch (start us, length us, event | category | flops | bytes accessed | tf_op | source)
XLA Modules:
  0.0 412.9 jit_solution(14278772960810796945)
XLA Ops:
  0.7 5.8 %fusion = f32[512,512]{1,0:T(8,128)} fusion(bf16[3072,512]{1,0:T(8,128)(2,1)} %param.9, f32[3072]{0:T(1024)} %param.12), kind=kOutput, calls=%fused_computation.5 | convolution fusion | flops 1615331328 | bytes 4206592 | tf_op jit(solution)/shard_map/dot_general | solution.py:34
  6.5 2.7 copy.12
  9.2 1.7 bitcast_add_fusion
  11.0 2.3 broadcast_select_fusion
  18.3 2.1 select_n.159
  21.8 2.4 collective-permute-start.5
  24.3 5.2 %collective-permute-start.6 = (f32[1328]{0:T(1024)}, f32[1328]{0:T(1024)}, u32[]{:S(2)}, u32[]{:S(2)}) collective-permute-start(f32[1328]{0:T(1024)} %param.13), channel_id=1, source_target_pairs={{2,0},{4,2},{6,4},{8,6},{10,8},{12,10},{14,12},{16,14},{18,16},{20... | collective-permute-start | bytes 15944 | tf_op jit(solution)/shard_map/ppermute | solution.py:22
  29.5 2.1 select_n.157
  31.6 9.3 %collective-permute-done.1 = f32[1536,128]{1,0:T(8,128)} collective-permute-done((f32[1536,128]{1,0:T(8,128)}, f32[1536,128]{1,0:T(8,128)}, u32[]{:S(2)}, u32[]{:S(2)}) %collective-permute-start.1) | collective-permute-done | bytes 786464 | tf_op jit(solution)/shard_map/ppermute | solution.py:138
  46.9 17.3 %scatter_custom_fusion = f32[3984]{0:T(1024)} fusion(s32[3072]{0:T(1024)} %get-tuple-element.15, f32[3072]{0:T(1024)S(1)} %copy-done.19, f32[]{:T(128)} %constant.79.clone.1), kind=kCustom, calls=%fused_computation.177 | custom fusion | flops 3072 | bytes 16448 | tf_op jit(solution)/shard_map/scatter-add | solution.py:172
  66.9 30.6 %gather_fusion = f32[3072]{0:T(1024)} fusion(f32[3984]{0:T(1024)S(1)} %concatenate.75, s32[3072]{0:T(1024)} %get-tuple-element.14), kind=kCustom, calls=%fused_computation | custom fusion | bytes 36864 | tf_op jit(solution)/shard_map/jit(_take)/gather | solution.py:156
  100.3 5.4 %collective-permute-done.3 = f32[384,128]{1,0:T(8,128)S(1)} collective-permute-done((f32[384,128]{1,0:T(8,128)S(1)}, f32[384,128]{1,0:T(8,128)S(1)}, u32[]{:S(2)}, u32[]{:S(2)}) %collective-permute-start.3) | collective-permute-done | bytes 196640 | tf_op jit(solution)/shard_map/ppermute | solution.py:138
  105.9 2.7 collective-permute-start.4
  108.5 3.1 collective-permute-done.4
  111.6 3.4 collective-permute-start.7
  115.1 2.6 collective-permute-done.7
  117.8 5.7 %collective-permute-done.8 = f32[400,128]{1,0:T(8,128)S(1)} collective-permute-done((f32[400,128]{1,0:T(8,128)S(1)}, f32[400,128]{1,0:T(8,128)S(1)}, u32[]{:S(2)}, u32[]{:S(2)}) %collective-permute-start.8) | collective-permute-done | bytes 204832 | tf_op jit(solution)/shard_map/ppermute | solution.py:143
  124.1 7.6 %collective-permute-done.9 = f32[800,128]{1,0:T(8,128)S(1)} collective-permute-done((f32[800,128]{1,0:T(8,128)S(1)}, f32[800,128]{1,0:T(8,128)S(1)}, u32[]{:S(2)}, u32[]{:S(2)}) %collective-permute-start.9) | collective-permute-done | bytes 409632 | tf_op jit(solution)/shard_map/ppermute | solution.py:143
  133.2 13.4 %collective-permute-done.10 = f32[1600,128]{1,0:T(8,128)S(1)} collective-permute-done((f32[1600,128]{1,0:T(8,128)S(1)}, f32[1600,128]{1,0:T(8,128)S(1)}, u32[]{:S(2)}, u32[]{:S(2)}) %collective-permute-start.10) | collective-permute-done | bytes 819232 | tf_op jit(solution)/shard_map/ppermute | solution.py:143
  148.2 5.2 %concatenate.82 = f32[3080,128]{1,0:T(8,128)} concatenate(f32[3072,128]{1,0:T(8,128)} %bitcast.232, f32[4,128]{1,0:T(4,128)S(1)} %slice_reduce_fusion, f32[4,128]{1,0:T(4,128)S(1)} %bitcast.250), dimensions={0} | concatenate | bytes 3153920 | tf_op jit(solution)/shard_map/concatenate | solution.py:190
  153.3 3.8 collective-permute-done.11
  157.1 2.1 broadcast_select_fusion.2
  160.9 1.8 fusion.3
  162.7 4.6 %reshape.72 = f32[2,512,768]{2,1,0:T(8,128)} reshape(f32[2,3072,128]{2,1,0:T(8,128)} %fusion.3) | data formatting | bytes 6291456 | tf_op jit(solution)/shard_map/reshape | solution.py:193
  167.4 1.9 slice_bitcast_fusion
  171.8 2.3 select_maximum_fusion
  174.1 15.3 %shard_map.86 = f32[128,128]{1,0:T(8,128)} custom-call(f32[128,128]{1,0:T(8,128)} %slice.336.a_ref), custom_call_target="tpu_custom_call" | custom-call | flops 8388608 | bytes 131072 | tf_op jit(solution)/shard_map/pallas_call | solution.py:71
  189.4 1.9 fusion.28
  191.3 5.4 %slice_subtract_fusion = f32[904,896]{1,0:T(8,128)S(1)} fusion(f32[1032,1024]{1,0:T(8,128)} %select_maximum_fusion, f32[904,128]{1,0:T(8,128)S(1)} %fusion.28), kind=kOutput, calls=%fused_computation.17 | convolution fusion | flops 1244945408 | bytes 7401472 | tf_op jit(solution)/shard_map/dot_general | solution.py:40
  199.0 15.3 %shard_map.87 = f32[128,128]{1,0:T(8,128)} custom-call(f32[128,128]{1,0:T(8,128)} %slice.343.a_ref), custom_call_target="tpu_custom_call" | custom-call | flops 8388608 | bytes 131072 | tf_op jit(solution)/shard_map/pallas_call | solution.py:71
  214.4 1.8 fusion.33
  216.2 3.8 slice_subtract_fusion.1
  222.0 15.3 %shard_map.88 = f32[128,128]{1,0:T(8,128)} custom-call(f32[128,128]{1,0:T(8,128)} %slice.348.a_ref), custom_call_target="tpu_custom_call" | custom-call | flops 8388608 | bytes 131072 | tf_op jit(solution)/shard_map/pallas_call | solution.py:71
  237.4 1.7 fusion.38
  239.8 3.2 slice_subtract_fusion.2
  244.8 15.3 %shard_map.89 = f32[128,128]{1,0:T(8,128)} custom-call(f32[128,128]{1,0:T(8,128)} %slice.353.a_ref), custom_call_target="tpu_custom_call" | custom-call | flops 8388608 | bytes 131072 | tf_op jit(solution)/shard_map/pallas_call | solution.py:71
  262.3 2.3 convolution_subtract_fusion
  266.3 15.3 %shard_map.90 = f32[128,128]{1,0:T(8,128)} custom-call(f32[128,128]{1,0:T(8,128)} %slice.358.a_ref), custom_call_target="tpu_custom_call" | custom-call | flops 8388608 | bytes 131072 | tf_op jit(solution)/shard_map/pallas_call | solution.py:71
  283.7 1.9 convolution_subtract_fusion.1
  287.0 15.3 %shard_map.91 = f32[128,128]{1,0:T(8,128)} custom-call(f32[128,128]{1,0:T(8,128)} %slice.363.a_ref), custom_call_target="tpu_custom_call" | custom-call | flops 8388608 | bytes 131072 | tf_op jit(solution)/shard_map/pallas_call | solution.py:71
  307.0 15.3 %shard_map.92 = f32[128,128]{1,0:T(8,128)} custom-call(f32[128,128]{1,0:T(8,128)} %slice.368.a_ref), custom_call_target="tpu_custom_call" | custom-call | flops 8388608 | bytes 131072 | tf_op jit(solution)/shard_map/pallas_call | solution.py:71
  326.5 15.3 %shard_map.93 = f32[128,128]{1,0:T(8,128)} custom-call(f32[128,128]{1,0:T(8,128)} %slice.373.a_ref), custom_call_target="tpu_custom_call" | custom-call | flops 8388608 | bytes 131072 | tf_op jit(solution)/shard_map/pallas_call | solution.py:71
  376.8 3.6 collective-permute-start.15
  380.4 2.2 collective-permute-start.16
  382.7 16.7 %scatter_custom_fusion.1 = f32[3984]{0:T(1024)S(1)} fusion(s32[3072]{0:T(1024)} %get-tuple-element.15, f32[3072]{0:T(1024)S(1)} %multiply_subtract_fusion, f32[]{:T(128)} %constant.79.clone.1), kind=kCustom, calls=%fused_computation.175 | custom fusion | flops 3072 | bytes 16448 | tf_op jit(solution)/shard_map/scatter-add | solution.py:210
  399.5 5.4 %collective-permute-start.13 = (f32[1328]{0:T(1024)S(1)}, f32[1328]{0:T(1024)S(1)}, u32[]{:S(2)}, u32[]{:S(2)}) collective-permute-start(f32[1328]{0:T(1024)S(1)} %get-tuple-element.38), channel_id=1, source_target_pairs={{2,0},{4,2},{6,4},{8,6},{10,8},{12,10},{14,12},{16,14},{18,16},{20... | collective-permute-start | bytes 15944 | tf_op jit(solution)/shard_map/ppermute | solution.py:30
  404.9 1.9 collective-permute-start.14
  407.5 4.7 %collective-permute-done.14 = f32[1328]{0:T(1024)S(1)} collective-permute-done((f32[1328]{0:T(1024)S(1)}, f32[1328]{0:T(1024)S(1)}, u32[]{:S(2)}, u32[]{:S(2)}) %collective-permute-start.14) | collective-permute-done | bytes 5344 | tf_op jit(solution)/shard_map/ppermute | solution.py:30
  (178 shorter events, 84.5 us)
Async XLA Ops:
  0.6 10.3 %collective-permute-start = (bf16[3072,512]{1,0:T(8,128)(2,1)}, bf16[3072,512]{1,0:T(8,128)(2,1)}, u32[]{:S(2)}, u32[]{:S(2)}) collective-permute-start(bf16[3072,512]{1,0:T(8,128)(2,1)} %param.9), channel_id=1, source_target_pairs={{0,1},{1,0},{2,3},{3,2},{4,5},{5,4},{6,7},{7,6},{8,9},{9,8},{10,11... | collective-permute-start | bytes 9437192 | tf_op jit(solution)/shard_map/ppermute | solution.py:115
  6.5 4.5 %copy-start = (bf16[3072,512]{1,0:T(8,128)(2,1)S(1)}, bf16[3072,512]{1,0:T(8,128)(2,1)}, u32[]{:S(2)}) copy-start(bf16[3072,512]{1,0:T(8,128)(2,1)} %param.9) | copy-start | bytes 9437188
  10.9 2.3 copy-start.19
  20.4 20.5 %collective-permute-start.1 = (f32[1536,128]{1,0:T(8,128)}, f32[1536,128]{1,0:T(8,128)}, u32[]{:S(2)}, u32[]{:S(2)}) collective-permute-start(f32[1536,128]{1,0:T(8,128)} %select_n.159), channel_id=1, source_target_pairs={{0,2},{2,0},{4,6},{6,4},{8,10},{10,8},{12,14},{14,12},{16,18},{18,... | collective-permute-start | bytes 2359304 | tf_op jit(solution)/shard_map/ppermute | solution.py:138
  21.8 44.2 %collective-permute-start.5 = (f32[1328]{0:T(1024)}, f32[1328]{0:T(1024)}, u32[]{:S(2)}, u32[]{:S(2)}) collective-permute-start(f32[1328]{0:T(1024)} %param.13), channel_id=1, source_target_pairs={{0,2},{2,4},{4,6},{6,8},{8,10},{10,12},{12,14},{14,16},{16,18},{18... | collective-permute-start | bytes 15944 | tf_op jit(solution)/shard_map/ppermute | solution.py:19
  24.3 41.8 %collective-permute-start.6 = (f32[1328]{0:T(1024)}, f32[1328]{0:T(1024)}, u32[]{:S(2)}, u32[]{:S(2)}) collective-permute-start(f32[1328]{0:T(1024)} %param.13), channel_id=1, source_target_pairs={{2,0},{4,2},{6,4},{8,6},{10,8},{12,10},{14,12},{16,14},{18,16},{20... | collective-permute-start | bytes 15944 | tf_op jit(solution)/shard_map/ppermute | solution.py:22
  42.3 0.9 copy-start.8
  44.0 54.3 %collective-permute-start.2 = (f32[768,128]{1,0:T(8,128)}, f32[768,128]{1,0:T(8,128)S(1)}, u32[]{:S(2)}, u32[]{:S(2)}) collective-permute-start(f32[768,128]{1,0:T(8,128)} %slice_select_fusion), channel_id=1, source_target_pairs={{0,4},{2,6},{4,0},{6,2},{8,12},{10,14},{12,8},{14,10},{16,20},{18,... | collective-permute-start | bytes 1179656 | tf_op jit(solution)/shard_map/ppermute | solution.py:138
  99.5 6.3 %collective-permute-start.3 = (f32[384,128]{1,0:T(8,128)S(1)}, f32[384,128]{1,0:T(8,128)S(1)}, u32[]{:S(2)}, u32[]{:S(2)}) collective-permute-start(f32[384,128]{1,0:T(8,128)S(1)} %slice_select_fusion.1), channel_id=1, source_target_pairs={{0,8},{2,10},{4,12},{6,14},{8,0},{10,2},{12,4},{14,6},{16,24},{18,... | collective-permute-start | bytes 589832 | tf_op jit(solution)/shard_map/ppermute | solution.py:138
  105.9 5.7 %collective-permute-start.4 = (f32[192,128]{1,0:T(8,128)S(1)}, f32[192,128]{1,0:T(8,128)S(1)}, u32[]{:S(2)}, u32[]{:S(2)}) collective-permute-start(f32[192,128]{1,0:T(8,128)S(1)} %slice_select_fusion.2), channel_id=1, source_target_pairs={{0,16},{2,18},{4,20},{6,22},{8,24},{10,26},{12,28},{14,30},{16,0},... | collective-permute-start | bytes 294920 | tf_op jit(solution)/shard_map/ppermute | solution.py:138
  111.6 6.1 %collective-permute-start.7 = (f32[200,128]{1,0:T(8,128)S(1)}, f32[200,128]{1,0:T(8,128)S(1)}, u32[]{:S(2)}, u32[]{:S(2)}) collective-permute-start(f32[200,128]{1,0:T(8,128)S(1)} %pad_maximum_fusion.5), channel_id=1, source_target_pairs={{0,16},{2,18},{4,20},{6,22},{8,24},{10,26},{12,28},{14,30},{16,0},... | collective-permute-start | bytes 307208 | tf_op jit(solution)/shard_map/ppermute | solution.py:143
  117.7 5.8 %collective-permute-start.8 = (f32[400,128]{1,0:T(8,128)S(1)}, f32[400,128]{1,0:T(8,128)S(1)}, u32[]{:S(2)}, u32[]{:S(2)}) collective-permute-start(f32[400,128]{1,0:T(8,128)S(1)} %pad_maximum_fusion.4), channel_id=1, source_target_pairs={{0,8},{2,10},{4,12},{6,14},{8,0},{10,2},{12,4},{14,6},{16,24},{18,... | collective-permute-start | bytes 614408 | tf_op jit(solution)/shard_map/ppermute | solution.py:143
  123.6 8.0 %collective-permute-start.9 = (f32[800,128]{1,0:T(8,128)S(1)}, f32[800,128]{1,0:T(8,128)S(1)}, u32[]{:S(2)}, u32[]{:S(2)}) collective-permute-start(f32[800,128]{1,0:T(8,128)S(1)} %pad_maximum_fusion.3), channel_id=1, source_target_pairs={{0,4},{2,6},{4,0},{6,2},{8,12},{10,14},{12,8},{14,10},{16,20},{18,... | collective-permute-start | bytes 1228808 | tf_op jit(solution)/shard_map/ppermute | solution.py:143
  131.8 14.8 %collective-permute-start.10 = (f32[1600,128]{1,0:T(8,128)S(1)}, f32[1600,128]{1,0:T(8,128)S(1)}, u32[]{:S(2)}, u32[]{:S(2)}) collective-permute-start(f32[1600,128]{1,0:T(8,128)S(1)} %pad_maximum_fusion.1), channel_id=1, source_target_pairs={{0,2},{2,0},{4,6},{6,4},{8,10},{10,8},{12,14},{14,12},{16,18},{18,... | collective-permute-start | bytes 2457608 | tf_op jit(solution)/shard_map/ppermute | solution.py:143
  146.7 1.5 copy-start.25
  153.3 3.8 collective-permute-start.11
  159.2 1.2 copy-start.1
  159.2 1.7 copy-start.3
  167.4 3.2 copy-start.2
  167.4 3.2 copy-start.4
  191.3 5.4 %copy-start.7 = (f32[904,128]{1,0:T(8,128)}, f32[904,128]{1,0:T(8,128)S(1)}, u32[]{:S(2)}) copy-start(f32[904,128]{1,0:T(8,128)S(1)} %fusion.28) | copy-start | bytes 1388548
  196.8 1.7 copy-start.5
  220.0 1.4 copy-start.6
  239.1 0.7 copy-start.10
  242.9 1.2 copy-start.9
  261.6 0.7 copy-start.11
  264.7 1.0 copy-start.12
  283.1 0.7 copy-start.13
  285.6 0.8 copy-start.15
  303.7 0.7 copy-start.14
  305.7 0.7 copy-start.17
  323.5 0.6 copy-start.16
  325.3 0.6 copy-start.18
  341.9 34.8 %copy-start.21 = (f32[3984]{0:T(1024)S(1)}, f32[3984]{0:T(1024)}, u32[]{:S(2)}) copy-start(f32[3984]{0:T(1024)} %scatter_custom_fusion) | copy-start | bytes 47812
  341.9 40.8 %copy-start.20 = (f32[3072]{0:T(1024)S(1)}, f32[3072]{0:T(1024)}, u32[]{:S(2)}) copy-start(f32[3072]{0:T(1024)} %param.12) | copy-start | bytes 36868
  341.9 40.8 %copy-start.23 = (s32[3072]{0:T(1024)S(1)}, s32[3072]{0:T(1024)}, u32[]{:S(2)}) copy-start(s32[3072]{0:T(1024)} %param.11) | copy-start | bytes 36868
  362.3 49.9 %copy-start.22 = (f32[3984]{0:T(1024)S(1)}, f32[3984]{0:T(1024)}, u32[]{:S(2)}) copy-start(f32[3984]{0:T(1024)} %scatter_custom_fusion) | copy-start | bytes 47812
  362.3 49.9 %copy-start.24 = (f32[1328]{0:T(1024)S(1)}, f32[1328]{0:T(1024)}, u32[]{:S(2)}) copy-start(f32[1328]{0:T(1024)} %param.15) | copy-start | bytes 15940
  376.5 6.1 %collective-permute-start.12 = (f32[3072]{0:T(1024)S(1)}, f32[3072]{0:T(1024)S(1)}, u32[]{:S(2)}, u32[]{:S(2)}) collective-permute-start(f32[3072]{0:T(1024)S(1)} %bitcast.241), channel_id=1, source_target_pairs={{0,1},{1,0},{2,3},{3,2},{4,5},{5,4},{6,7},{7,6},{8,9},{9,8},{10,11... | collective-permute-start | bytes 36872 | tf_op jit(solution)/shard_map/ppermute | solution.py:125
  376.8 30.7 %collective-permute-start.15 = (f32[1328]{0:T(1024)S(1)}, f32[1328]{0:T(1024)S(1)}, u32[]{:S(2)}, u32[]{:S(2)}) collective-permute-start(f32[1328]{0:T(1024)S(1)} %get-tuple-element.36), channel_id=1, source_target_pairs={{2,0},{4,2},{6,4},{8,6},{10,8},{12,10},{14,12},{16,14},{18,16},{20... | collective-permute-start | bytes 15944 | tf_op jit(solution)/shard_map/ppermute | solution.py:30
  380.4 27.1 %collective-permute-start.16 = (f32[1328]{0:T(1024)S(1)}, f32[1328]{0:T(1024)S(1)}, u32[]{:S(2)}, u32[]{:S(2)}) collective-permute-start(f32[1328]{0:T(1024)S(1)} %get-tuple-element.37), channel_id=1, source_target_pairs={{0,2},{2,4},{4,6},{6,8},{8,10},{10,12},{12,14},{14,16},{16,18},{18... | collective-permute-start | bytes 15944 | tf_op jit(solution)/shard_map/ppermute | solution.py:30
  399.5 8.0 %collective-permute-start.13 = (f32[1328]{0:T(1024)S(1)}, f32[1328]{0:T(1024)S(1)}, u32[]{:S(2)}, u32[]{:S(2)}) collective-permute-start(f32[1328]{0:T(1024)S(1)} %get-tuple-element.38), channel_id=1, source_target_pairs={{2,0},{4,2},{6,4},{8,6},{10,8},{12,10},{14,12},{16,14},{18,16},{20... | collective-permute-start | bytes 15944 | tf_op jit(solution)/shard_map/ppermute | solution.py:30
  404.9 7.3 %collective-permute-start.14 = (f32[1328]{0:T(1024)S(1)}, f32[1328]{0:T(1024)S(1)}, u32[]{:S(2)}, u32[]{:S(2)}) collective-permute-start(f32[1328]{0:T(1024)S(1)} %get-tuple-element.39), channel_id=1, source_target_pairs={{0,2},{2,4},{4,6},{6,8},{8,10},{10,12},{12,14},{14,16},{16,18},{18... | collective-permute-start | bytes 15944 | tf_op jit(solution)/shard_map/ppermute | solution.py:30
